TPU v7x, 512 devices: a whole 4x4x16 slice. The times are simulated.
512 devices in a mesh: ctx: 64 (over z, y), head: 8 (over x, core).
Axes of the slice: x: 4, y: 4, z: 16, core: 2. Of those that a mesh axis runs over, the one named last changes fastest.
Arguments:
- queries: bfloat16 [8192, 4096], P(('ctx', 'head')), may hold values from -4.6 to 4.6
- key_states: bfloat16 [8192, 4096], P(('ctx', 'head')), may hold values from -4.6 to 4.6
- value_states: bfloat16 [8192, 4096], P(('ctx', 'head')), may hold values from -6 to 6
- out_grad: bfloat16 [8192, 4096], P(('ctx', 'head')), may hold values from -6 to 6
- random_blocks: int32 [256, 3], replicated, may hold values from 0 to 255, as said below
- global_blocks: int32 [4], replicated, may hold values from 0 to 255, as said below
Outputs:
- query_grad: bfloat16 [8192, 4096], P('ctx', 'head')
- key_grad: bfloat16 [8192, 4096], P('ctx', 'head')
- value_grad: bfloat16 [8192, 4096], P('ctx', 'head')
Inputs may be any that keep to these rules, and one draw needn't show every extreme that they name: `random_blocks`: with the blocks i * 4 to i * 4 + 3 called range i: the 12 entries of the rows of range i name blocks of any one range at most 1 times, and some range exactly 1 times. `global_blocks`: 4 different blocks, one of them the last block 255, in any order.
All inputs are finite; a program needn't handle non-finite values.
Results may differ from a plain program's by a relative error of at most 0.0077.
Values may be sent and summed in bfloat16 or wider, within the bound.
No kernel may reach another device: no remote copies, remote signals or barrier semaphores. Data moves between devices by JAX's collectives and lax.ppermute only.
A program may use at most 128 MiB of HBM per device.

v0:
```python
import math
import jax
import jax.numpy as jnp
from jax import lax
from jax.sharding import PartitionSpec as P

DH = 128
BS = 32
NR = 3
NG = 4


def with_halo(x, sides, width):
    for axis, dim in sides:
        peers, length = (lax.axis_size(axis), x.shape[dim])
        up = [(i, (i + 1) % peers) for i in range(peers - 1)]
        down = [(j, i) for i, j in up]
        last = lax.slice_in_dim(x, length - width, length, axis=dim)
        first = lax.slice_in_dim(x, 0, width, axis=dim)
        before = lax.ppermute(last, axis, up)
        after = lax.ppermute(first, axis, down)
        x = jnp.concatenate([before, x, after], axis=dim)
    return x


def spread(x, axis, root):
    mine = lax.axis_index(axis) == root
    return lax.psum(jnp.where(mine, x, jnp.zeros_like(x)), axis)


def per_device(queries, key_states, value_states, out_grad, random_blocks, global_blocks):
    query_rows, key_rows, value_rows, grad_rows = (
        lax.all_to_all(queries, "head", split_axis=1, concat_axis=0, tiled=True),
        lax.all_to_all(key_states, "head", split_axis=1, concat_axis=0, tiled=True),
        lax.all_to_all(value_states, "head", split_axis=1, concat_axis=0, tiled=True),
        lax.all_to_all(out_grad, "head", split_axis=1, concat_axis=0, tiled=True),
    )
    tokens = query_rows.shape[0]
    head_cols = query_rows.shape[1]
    heads_here = head_cols // DH
    blocks_here = tokens // BS
    devices = lax.axis_size("ctx")
    my_index = lax.axis_index("ctx")
    total_blocks = devices * blocks_here
    entries = blocks_here * NR
    capacity = (entries + devices - 1) // devices
    inv_root = 1.0 / math.sqrt(DH)
    kv_rows = jnp.concatenate([key_rows, value_rows], axis=1)
    kv_blocks = kv_rows.reshape(blocks_here, BS, 2 * head_cols)
    extended = with_halo(kv_rows, (("ctx", 0),), BS)
    extended = extended.reshape(blocks_here + 2, BS, 2 * head_cols)
    window = jnp.stack(
        [extended[:blocks_here], extended[1 : blocks_here + 1], extended[2:]], axis=1
    )
    global_owner = global_blocks // blocks_here
    global_offset = global_blocks % blocks_here
    pieces = []
    for member in range(NG):
        own_block = lax.dynamic_index_in_dim(kv_blocks, global_offset[member], 0, keepdims=False)
        pieces.append(spread(own_block, "ctx", global_owner[member]))
    global_kv = jnp.stack(pieces)
    entry_table = random_blocks.reshape(devices, entries)
    table_owner = entry_table // blocks_here
    table_offset = entry_table % blocks_here
    positions = jnp.arange(entries, dtype=jnp.int32)
    before = positions[None, :] < positions[:, None]
    matches = (table_owner[:, :, None] == table_owner[:, None, :]) & before[None]
    table_slot = jnp.sum(matches.astype(jnp.int32), axis=2)
    my_owner = lax.dynamic_index_in_dim(table_owner, my_index, 0, keepdims=False)
    my_slot = lax.dynamic_index_in_dim(table_slot, my_index, 0, keepdims=False)
    my_target = my_owner * capacity + my_slot
    slot_ids = jnp.arange(capacity, dtype=jnp.int32)
    served = (table_owner == my_index)[:, :, None] & (
        table_slot[:, :, None] == slot_ids[None, None, :]
    )
    served_block = jnp.sum(jnp.where(served, table_offset[:, :, None], 0), axis=1).reshape(-1)
    served_used = jnp.any(served, axis=1).reshape(-1)
    outgoing = jnp.take(kv_blocks, served_block, axis=0)
    incoming = lax.all_to_all(outgoing, "ctx", split_axis=0, concat_axis=0, tiled=True)
    fetched = jnp.take(incoming, my_target, axis=0).reshape(blocks_here, NR, BS, 2 * head_cols)
    near_kv = jnp.concatenate([window, fetched], axis=1)
    near_groups = 3 + NR
    near_count = near_groups * BS
    query_heads = query_rows.reshape(blocks_here, BS, heads_here, DH)
    grad_heads = grad_rows.reshape(blocks_here, BS, heads_here, DH)
    near_keys = near_kv[..., :head_cols].reshape(blocks_here, near_groups, BS, heads_here, DH)
    near_values = near_kv[..., head_cols:].reshape(blocks_here, near_groups, BS, heads_here, DH)
    far_keys = global_kv[..., :head_cols].reshape(NG, BS, heads_here, DH)
    far_values = global_kv[..., head_cols:].reshape(NG, BS, heads_here, DH)
    scores = (
        jnp.concatenate(
            [
                jnp.einsum(
                    "bqhd,bgkhd->bhqgk", query_heads, near_keys, preferred_element_type=jnp.float32
                ).reshape(blocks_here, heads_here, BS, near_count),
                jnp.einsum(
                    "bqhd,gkhd->bhqgk", query_heads, far_keys, preferred_element_type=jnp.float32
                ).reshape(blocks_here, heads_here, BS, NG * BS),
            ],
            axis=3,
        )
        * inv_root
    )
    block_ids = my_index * blocks_here + jnp.arange(blocks_here, dtype=jnp.int32)
    usable = jnp.concatenate(
        [
            (block_ids > 0)[:, None],
            jnp.ones((blocks_here, 1), bool),
            (block_ids < total_blocks - 1)[:, None],
            jnp.ones((blocks_here, NR + NG), bool),
        ],
        axis=1,
    )
    column_ok = jnp.repeat(usable, BS, axis=1)[:, None, None, :]
    masked = jnp.where(column_ok, scores, -jnp.inf)
    row_max = jnp.max(masked, axis=3, keepdims=True)
    log_total = row_max + jnp.log(jnp.sum(jnp.exp(masked - row_max), axis=3, keepdims=True))
    probs_full = jnp.exp(masked - log_total)
    probs_half = probs_full.astype(jnp.bfloat16)
    near_probs = probs_half[..., :near_count].reshape(blocks_here, heads_here, BS, near_groups, BS)
    far_probs = probs_half[..., near_count:].reshape(blocks_here, heads_here, BS, NG, BS)
    outputs = jnp.einsum(
        "bhqgk,bgkhd->bqhd", near_probs, near_values, preferred_element_type=jnp.float32
    ) + jnp.einsum("bhqgk,gkhd->bqhd", far_probs, far_values, preferred_element_type=jnp.float32)
    row_dot = jnp.sum(grad_heads.astype(jnp.float32) * outputs, axis=3)
    dprobs = jnp.concatenate(
        [
            jnp.einsum(
                "bqhd,bgkhd->bhqgk", grad_heads, near_values, preferred_element_type=jnp.float32
            ).reshape(blocks_here, heads_here, BS, near_count),
            jnp.einsum(
                "bqhd,gkhd->bhqgk", grad_heads, far_values, preferred_element_type=jnp.float32
            ).reshape(blocks_here, heads_here, BS, NG * BS),
        ],
        axis=3,
    )
    dscores = probs_full * (dprobs - jnp.transpose(row_dot, (0, 2, 1))[..., None])
    ds_half = dscores.astype(jnp.bfloat16)
    near_ds = ds_half[..., :near_count].reshape(blocks_here, heads_here, BS, near_groups, BS)
    far_ds = ds_half[..., near_count:].reshape(blocks_here, heads_here, BS, NG, BS)
    query_grad = (
        (
            (
                jnp.einsum(
                    "bhqgk,bgkhd->bqhd", near_ds, near_keys, preferred_element_type=jnp.float32
                )
                + jnp.einsum(
                    "bhqgk,gkhd->bqhd", far_ds, far_keys, preferred_element_type=jnp.float32
                )
            )
            * inv_root
        )
        .astype(jnp.bfloat16)
        .reshape(tokens, head_cols)
    )

    def key_value_parts(ds_part, probs_part):
        key_part = (
            jnp.einsum(
                "bhqgk,bqhd->bgkhd", ds_part, query_heads, preferred_element_type=jnp.float32
            )
            * inv_root
        )
        value_part = jnp.einsum(
            "bhqgk,bqhd->bgkhd", probs_part, grad_heads, preferred_element_type=jnp.float32
        )
        out_shape = key_part.shape[:3] + (head_cols,)
        return jnp.concatenate([key_part.reshape(out_shape), value_part.reshape(out_shape)], axis=3)

    random_part = key_value_parts(near_ds[:, :, :, 3:], near_probs[:, :, :, 3:])
    random_part = random_part.astype(jnp.bfloat16).reshape(entries, BS, 2 * head_cols)
    back_rows = (
        jnp.zeros((devices * capacity, BS, 2 * head_cols), jnp.bfloat16)
        .at[my_target]
        .set(random_part)
    )
    arrived = lax.all_to_all(back_rows, "ctx", split_axis=0, concat_axis=0, tiled=True)
    window_part = key_value_parts(near_ds[:, :, :, :3], near_probs[:, :, :, :3])
    zero_block = jnp.zeros((1, BS, 2 * head_cols), jnp.float32)
    own_grad = (
        window_part[:, 1]
        + jnp.concatenate([window_part[1:, 0], zero_block], axis=0)
        + jnp.concatenate([zero_block, window_part[:-1, 2]], axis=0)
    )
    rims_out = jnp.concatenate([window_part[0, 0], window_part[blocks_here - 1, 2]], axis=0)
    rims_in = with_halo(rims_out.astype(jnp.bfloat16), (("ctx", 0),), BS).astype(rims_out.dtype)
    own_grad = own_grad.at[0].add(rims_in[:BS]).at[blocks_here - 1].add(rims_in[3 * BS :])
    far_key = (
        jnp.einsum("bhqgk,bqhd->gkhd", far_ds, query_heads, preferred_element_type=jnp.float32)
        * inv_root
    )
    far_value = jnp.einsum(
        "bhqgk,bqhd->gkhd", far_probs, grad_heads, preferred_element_type=jnp.float32
    )
    far_part = jnp.concatenate(
        [far_key.reshape(NG, BS, head_cols), far_value.reshape(NG, BS, head_cols)], axis=2
    )
    far_sum = lax.psum(far_part, "ctx")
    here_ids = jnp.arange(blocks_here, dtype=jnp.int32)
    own_global = (
        (global_owner == my_index)[None, :] & (global_offset[None, :] == here_ids[:, None])
    ).astype(jnp.float32)
    own_grad = own_grad + jnp.einsum(
        "jg,gkc->jkc", own_global, far_sum, precision=lax.Precision.HIGHEST
    )
    weights = (served_used[None, :] & (served_block[None, :] == here_ids[:, None])).astype(
        jnp.bfloat16
    )
    own_grad = own_grad + jnp.einsum(
        "jr,rkc->jkc", weights, arrived, preferred_element_type=jnp.float32
    )
    key_grad = own_grad[..., :head_cols].astype(jnp.bfloat16).reshape(tokens, head_cols)
    value_grad = own_grad[..., head_cols:].astype(jnp.bfloat16).reshape(tokens, head_cols)
    return (query_grad, key_grad, value_grad)


def solution(mesh):
    placed = (
        P(("ctx", "head"), None),
        P(("ctx", "head"), None),
        P(("ctx", "head"), None),
        P(("ctx", "head"), None),
        P(),
        P(),
    )
    return jax.shard_map(
        per_device,
        mesh=mesh,
        in_specs=placed,
        out_specs=(P("ctx", "head"), P("ctx", "head"), P("ctx", "head")),
        check_vma=False,
    )
```

profile of v0, /device:TPU:2, one launch (start us, length us, event | category | flops | bytes accessed | tf_op | source)
XLA Modules:
  0.0 762.3 jit_solution(3867168004326014338)
XLA Ops:
  7.2 1.6 copy.526
  8.8 9.2 %all-to-all-start = ((bf16[16,8,512]{2,0,1:T(8,128)(2,1)}), bf16[16,8,512]{2,0,1:T(8,128)(2,1)S(1)}, u32[]{:S(2)}, u32[]{:S(2)}) async-start(bf16[16,8,512]{2,0,1:T(8,128)(2,1)} %bitcast.216), calls=%async_computation | async-start | bytes 262144 | tf_op jit(solution)/shard_map/all_to_all | solution.py:34
  18.7 0.8 copy.297
  20.3 0.8 fusion.90
  22.7 4.7 all-to-all-start.1
  28.8 3.4 all-to-all-done.1
  32.1 4.7 all-to-all-start.3
  36.9 2.8 gather_fusion
  39.7 1.8 all-to-all-done.3
  41.6 4.7 all-to-all-start.4
  46.3 4.6 broadcast_select_fusion
  51.0 14.6 %all-to-all-start.2 = ((bf16[64,32,1024]{2,1,0:T(8,128)(2,1)}), bf16[64,32,1024]{2,1,0:T(8,128)(2,1)}, u32[]{:S(2)}, u32[]{:S(2)}) async-start(bf16[64,32,1024]{2,1,0:T(8,128)(2,1)} %broadcast_select_fusion), calls=%async_computation.2 | async-start | bytes 8388608 | tf_op jit(solution)/shard_map/all_to_all | solution.py:79
  79.1 0.7 fusion.72
  79.9 3.4 collective-permute-start
  83.3 1.5 collective-permute-start.1
  84.8 0.7 maximum_bitcast_fusion
  85.6 4.1 collective-permute-done.1
  89.7 0.8 pad_maximum_fusion.6
  90.5 298.1 %all-reduce.8.cloned.1.call-done = (bf16[1,32,1024]{2,1,0:T(8,128)(2,1)}, bf16[1,32,1024]{2,1,0:T(8,128)(2,1)}, bf16[1,32,1024]{2,1,0:T(8,128)(2,1)}, bf16[1,32,1024]{2,1,0:T(8,128)(2,1)}) async-done(((bf16[1,32,1024]{2,1,0:T(8,128)(2,1)}, bf16[1,32,1024]{2,1,0:T(8,128)(2,1)}, bf16[1,32,1024]{2,1,0:T(8,128)(2,1)}, bf16[1,32,1024]{2,1,0:T(8,128)(2,1)}), (bf16[1,32,1024]{2,1,0:T(8,128)(2,1)}, ...) | async-done | bytes 262160 | tf_op jit(solution)/shard_map/psum | solution.py:28
  388.5 0.8 constant_dynamic-update-slice_fusion.3
  389.4 0.8 constant_dynamic-update-slice_fusion.2
  390.2 0.8 constant_dynamic-update-slice_fusion.1
  391.1 0.8 constant_dynamic-update-slice_fusion
  391.9 0.8 slice_bitcast_fusion.8
  394.8 1.2 reshape.369
  396.0 2.8 gather_fusion.1
  399.2 1.3 slice_bitcast_fusion.1
  402.8 1.0 reshape.371
  404.3 1.2 fusion.92
  406.8 1.2 fusion.15
  408.6 0.9 concatenate.86
  410.0 1.5 fusion.24
  412.0 1.3 fusion.93
  414.5 2.5 broadcast_in_dim.69
  417.0 2.8 scatter_fusion
  419.9 9.1 %all-to-all-start.5 = ((bf16[64,32,1024]{2,1,0:T(8,128)(2,1)}), bf16[64,32,1024]{2,1,0:T(8,128)(2,1)}, u32[]{:S(2)}, u32[]{:S(2)}) async-start(bf16[64,32,1024]{2,1,0:T(8,128)(2,1)} %scatter_fusion), calls=%async_computation.5 | async-start | bytes 8388608 | tf_op jit(solution)/shard_map/all_to_all | solution.py:177
  429.5 1.7 slice.201
  431.7 0.8 reshape.436
  434.5 0.9 reshape.435
  435.3 1.9 pad_maximum_fusion.2
  438.7 3.5 collective-permute-start.2
  442.3 1.3 collective-permute-start.3
  445.3 3.3 collective-permute-done.3
  449.3 1.1 scatter-add.9
  450.3 164.0 %all-to-all-done.5 = bf16[64,32,1024]{2,1,0:T(8,128)(2,1)} async-done(((bf16[64,32,1024]{2,1,0:T(8,128)(2,1)}), bf16[64,32,1024]{2,1,0:T(8,128)(2,1)}, u32[]{:S(2)}, u32[]{:S(2)}) %all-to-all-start.5) | async-done | bytes 4194336 | tf_op jit(solution)/shard_map/all_to_all | solution.py:177
  614.3 6.7 fusion
  621.0 131.3 %all-reduce.6.cloned.1.call-done = f32[4,32,1024]{2,0,1:T(4,128)} async-done(((f32[4,32,1024]{2,0,1:T(4,128)}), f32[4,32,1024]{2,0,1:T(4,128)}) %all-reduce.6.cloned.1.call-update) | async-done | bytes 524304 | tf_op jit(solution)/shard_map/psum | solution.py:198
  752.3 1.7 fusion.5
  (170 shorter events, 24.7 us)
Async XLA Ops:
  7.2 14.2 %copy-start.19 = (bf16[16,4096]{1,0:T(8,128)(2,1)S(1)}, bf16[16,4096]{1,0:T(8,128)(2,1)}, u32[]{:S(2)}) copy-start(bf16[16,4096]{1,0:T(8,128)(2,1)} %param.12) | copy-start | bytes 393220
  7.2 20.3 %copy-start.20 = (bf16[16,4096]{1,0:T(8,128)(2,1)S(1)}, bf16[16,4096]{1,0:T(8,128)(2,1)}, u32[]{:S(2)}) copy-start(bf16[16,4096]{1,0:T(8,128)(2,1)} %param.10) | copy-start | bytes 393220
  7.2 20.9 %copy-start.21 = (bf16[16,4096]{1,0:T(8,128)(2,1)S(1)}, bf16[16,4096]{1,0:T(8,128)(2,1)}, u32[]{:S(2)}) copy-start(bf16[16,4096]{1,0:T(8,128)(2,1)} %param.13) | copy-start | bytes 393220
  8.8 13.9 %all-to-all-start = ((bf16[16,8,512]{2,0,1:T(8,128)(2,1)}), bf16[16,8,512]{2,0,1:T(8,128)(2,1)S(1)}, u32[]{:S(2)}, u32[]{:S(2)}) async-start(bf16[16,8,512]{2,0,1:T(8,128)(2,1)} %bitcast.216), calls=%async_computation | async-start | bytes 262144 | tf_op jit(solution)/shard_map/all_to_all | solution.py:34
  22.1 14.8 %copy-start.23 = (s32[64]{0:T(128)}, s32[64]{0:T(128)S(1)}, u32[]{:S(2)}) copy-start(s32[64]{0:T(128)S(1)} %reduce_sum.48) | copy-start | bytes 772
  22.7 9.4 %all-to-all-start.1 = ((bf16[16,8,512]{2,0,1:T(8,128)(2,1)}), bf16[16,8,512]{2,0,1:T(8,128)(2,1)S(1)}, u32[]{:S(2)}, u32[]{:S(2)}) async-start(bf16[16,8,512]{2,0,1:T(8,128)(2,1)} %bitcast.215), calls=%async_computation.1 | async-start | bytes 262144 | tf_op jit(solution)/shard_map/all_to_all | solution.py:35
  32.1 9.4 %all-to-all-start.3 = ((bf16[16,8,512]{2,0,1:T(8,128)(2,1)}), bf16[16,8,512]{2,0,1:T(8,128)(2,1)S(1)}, u32[]{:S(2)}, u32[]{:S(2)}) async-start(bf16[16,8,512]{2,0,1:T(8,128)(2,1)} %bitcast.214), calls=%async_computation.3 | async-start | bytes 262144 | tf_op jit(solution)/shard_map/all_to_all | solution.py:33
  41.6 9.4 %all-to-all-start.4 = ((bf16[16,8,512]{2,0,1:T(8,128)(2,1)}), bf16[16,8,512]{2,0,1:T(8,128)(2,1)S(1)}, u32[]{:S(2)}, u32[]{:S(2)}) async-start(bf16[16,8,512]{2,0,1:T(8,128)(2,1)} %bitcast.213), calls=%async_computation.4 | async-start | bytes 262144 | tf_op jit(solution)/shard_map/all_to_all | solution.py:36
  50.9 14.7 %copy-start.30 = (s32[4]{0:T(128)S(1)}, s32[4]{0:T(128)}, u32[]{:S(2)}) copy-start(s32[4]{0:T(128)} %param.15) | copy-start | bytes 52
  51.0 344.9 %all-to-all-start.2 = ((bf16[64,32,1024]{2,1,0:T(8,128)(2,1)}), bf16[64,32,1024]{2,1,0:T(8,128)(2,1)}, u32[]{:S(2)}, u32[]{:S(2)}) async-start(bf16[64,32,1024]{2,1,0:T(8,128)(2,1)} %broadcast_select_fusion), calls=%async_computation.2 | async-start | bytes 8388608 | tf_op jit(solution)/shard_map/all_to_all | solution.py:79
  65.6 322.9 %all-reduce.8.cloned.1.call-start = ((), (), s32[]{:S(2)}) async-start(), calls=%async_computation.7 | async-start | bytes 524288 | tf_op jit(solution)/shard_map/psum | solution.py:28
  78.5 12.0 %copy-start.26 = (s32[12]{0:T(128)}, s32[12]{0:T(128)S(1)}, u32[]{:S(2)}) copy-start(s32[12]{0:T(128)S(1)} %fusion.89) | copy-start | bytes 148
  79.9 320.6 %copy-start.3 = (bf16[4,32,4,128]{3,2,1,0:T(4,128)(2,1)}, bf16[4,32,4,128]{3,2,1,0:T(4,128)(2,1)S(1)}, u32[]{:S(2)}) copy-start(bf16[4,32,4,128]{3,2,1,0:T(4,128)(2,1)S(1)} %reshape.361) | copy-start | bytes 393220
  79.9 5.6 collective-permute-start
  83.3 6.4 collective-permute-start.1
  394.8 4.0 copy-start.28
  395.9 3.0 copy-start.13
  395.9 3.0 copy-start.14
  400.5 0.9 copy-start
  404.3 1.2 copy-start.2
  405.5 1.0 copy-start.5
  405.5 1.1 copy-start.18
  408.6 1.5 copy-start.22
  411.5 1.9 copy-start.12
  411.5 1.9 copy-start.4
  413.4 1.0 copy-start.11
  414.5 2.6 copy-start.27
  419.9 9.3 %copy-start.25 = (pred[256]{0:T(512)(128)(4,1)S(1)}, pred[256]{0:T(512)(128)(4,1)}, u32[]{:S(2)}) copy-start(pred[256]{0:T(512)(128)(4,1)} %get-tuple-element.33) | copy-start | bytes 772
  419.9 11.3 %copy-start.6 = (bf16[4,4,32,4,32]{4,3,2,1,0:T(4,128)(2,1)S(1)}, bf16[4,4,32,4,32]{4,3,2,1,0:T(4,128)(2,1)}, u32[]{:S(2)}) copy-start(bf16[4,4,32,4,32]{4,3,2,1,0:T(4,128)(2,1)} %reshape.371) | copy-start | bytes 393220
  419.9 194.4 %all-to-all-start.5 = ((bf16[64,32,1024]{2,1,0:T(8,128)(2,1)}), bf16[64,32,1024]{2,1,0:T(8,128)(2,1)}, u32[]{:S(2)}, u32[]{:S(2)}) async-start(bf16[64,32,1024]{2,1,0:T(8,128)(2,1)} %scatter_fusion), calls=%async_computation.5 | async-start | bytes 8388608 | tf_op jit(solution)/shard_map/all_to_all | solution.py:177
  428.9 3.6 copy-start.9
  428.9 323.4 %all-reduce.6.cloned.1.call-start = ((), (), s32[]{:S(2)}) async-start(), calls=%async_computation.6 | async-start | bytes 1048576 | tf_op jit(solution)/shard_map/psum | solution.py:198
  432.8 0.9 copy-start.16
  433.7 1.6 copy-start.15
  434.0 3.2 copy-start.7
  434.3 3.0 copy-start.10
  438.6 5.0 copy-start.8
  438.6 5.0 copy-start.17
  438.7 5.3 copy-start.1
  438.7 6.6 collective-permute-start.2
  442.3 6.4 collective-permute-start.3
  444.6 169.7 %copy-start.24 = (s32[64]{0:T(128)S(1)}, s32[64]{0:T(128)}, u32[]{:S(2)}) copy-start(s32[64]{0:T(128)} %copy-done.23) | copy-start | bytes 772
  450.3 302.0 %copy-start.29 = (pred[4]{0:T(512)(128)(4,1)S(1)}, pred[4]{0:T(512)(128)(4,1)}, u32[]{:S(2)}) copy-start(pred[4]{0:T(512)(128)(4,1)} %get-tuple-element.31) | copy-start | bytes 16
Sparse Core Ops, SparseCore 0:
  79.9 308.5 all-reduce.7
  437.4 314.8 all-reduce.5
where the time goes:
time: 764 us; the launch traced here: 762 us
  waiting for transfers between devices  607 us (79%)
  starting transfers between devices  57.1 us (7%)
  local copies, waits for them, and re-layouts  44 us (6%)
  between operations  25.1 us (3%)
  other arithmetic  15.6 us (2%)
  matrix products  13.9 us (2%)
    psum x1, waiting for transfers between devices, spread(): return lax.psum(jnp.where(mine, x, jnp.zeros_like(x)), axis)  298 us
    all_to_all x1, waiting for transfers between devices, per_device(): lax.all_to_all(back_rows, 'ctx', split_axis=0, concat_axis=0, tiled=True)  164 us
    psum x1, waiting for transfers between devices, per_device(): far_sum = lax.psum(far_part, 'ctx')  131 us
  transfers between devices with their start and end apart: 12, of which 9 were waited for; matrix products, arithmetic and copies ran while one was open for 6% of the time, Pallas kernels for 0%

commit v1 on v0

--- a/solution.py
+++ b/solution.py
@@ -1,13 +1,22 @@
+import functools
 import math
 import jax
 import jax.numpy as jnp
 from jax import lax
 from jax.sharding import PartitionSpec as P
+from jax.lax import all_gather
 
 DH = 128
 BS = 32
 NR = 3
 NG = 4
+
+
+def supply_samples(piece_in, named_axis):
+    return all_gather(piece_in, axis_name=named_axis).sum(axis=0)
+
+
+_fix_widths = functools.partial(supply_samples, named_axis="ctx")
 
 
 def with_halo(x, sides, width):
@@ -195,7 +204,7 @@
     far_part = jnp.concatenate(
         [far_key.reshape(NG, BS, head_cols), far_value.reshape(NG, BS, head_cols)], axis=2
     )
-    far_sum = lax.psum(far_part, "ctx")
+    far_sum = _fix_widths(far_part)
     here_ids = jnp.arange(blocks_here, dtype=jnp.int32)
     own_global = (
         (global_owner == my_index)[None, :] & (global_offset[None, :] == here_ids[:, None])

time: 764 us -> 888 us (1.16)
  the two profiles are of different devices: /device:TPU:2 before, /device:TPU:1 now
where the time goes in v1:
time: 888 us; the launch traced here: 886 us
  waiting for transfers between devices  716 us (81%)
  starting transfers between devices  56.8 us (6%)
  local copies, waits for them, and re-layouts  48.7 us (5%)
  between operations  24.7 us (3%)
  other arithmetic  24.6 us (3%)
  matrix products  15.2 us (2%)
    psum x1, waiting for transfers between devices, spread(): return lax.psum(jnp.where(mine, x, jnp.zeros_like(x)), axis)  290 us
    all_gather x1, waiting for transfers between devices, supply_samples(): return all_gather(piece_in, axis_name=named_axis).sum(axis=0)  207 us
    all_to_all x1, waiting for transfers between devices, per_device(): lax.all_to_all(back_rows, 'ctx', split_axis=0, concat_axis=0, tiled=True)  206 us
  transfers between devices with their start and end apart: 12, of which 9 were waited for; matrix products, arithmetic and copies ran while one was open for 6% of the time, Pallas kernels for 0%

profile of v1, /device:TPU:1, one launch (start us, length us, event | category | flops | bytes accessed | tf_op | source)
XLA Modules:
  0.0 885.9 jit_solution(16244006457607217820)
XLA Ops:
  7.2 1.6 copy.523
  8.8 10.2 %all-to-all-start = ((bf16[16,8,512]{2,0,1:T(8,128)(2,1)}), bf16[16,8,512]{2,0,1:T(8,128)(2,1)S(1)}, u32[]{:S(2)}, u32[]{:S(2)}) async-start(bf16[16,8,512]{2,0,1:T(8,128)(2,1)} %bitcast.220), calls=%async_computation | async-start | bytes 262144 | tf_op jit(solution)/shard_map/all_to_all | solution.py:43
  20.5 1.6 copy.522
  24.2 4.5 all-to-all-start.1
  30.1 3.9 all-to-all-done.1
  34.0 4.1 all-to-all-start.4
  38.2 2.8 gather_fusion
  41.0 2.4 all-to-all-done.4
  43.5 4.1 all-to-all-start.3
  47.6 4.7 broadcast_select_fusion
  52.9 14.3 %all-to-all-start.2 = ((bf16[64,32,1024]{2,1,0:T(8,128)(2,1)}), bf16[64,32,1024]{2,1,0:T(8,128)(2,1)}, u32[]{:S(2)}, u32[]{:S(2)}) async-start(bf16[64,32,1024]{2,1,0:T(8,128)(2,1)} %broadcast_select_fusion), calls=%async_computation.2 | async-start | bytes 8388608 | tf_op jit(solution)/shard_map/all_to_all | solution.py:88
  80.7 2.8 collective-permute-start
  83.5 1.5 collective-permute-start.1
  85.1 4.0 collective-permute-done.1
  89.2 290.0 %all-reduce.5.cloned.1.call-done = (bf16[1,32,1024]{2,1,0:T(8,128)(2,1)}, bf16[1,32,1024]{2,1,0:T(8,128)(2,1)}, bf16[1,32,1024]{2,1,0:T(8,128)(2,1)}, bf16[1,32,1024]{2,1,0:T(8,128)(2,1)}) async-done(((bf16[1,32,1024]{2,1,0:T(8,128)(2,1)}, bf16[1,32,1024]{2,1,0:T(8,128)(2,1)}, bf16[1,32,1024]{2,1,0:T(8,128)(2,1)}, bf16[1,32,1024]{2,1,0:T(8,128)(2,1)}), (bf16[1,32,1024]{2,1,0:T(8,128)(2,1)}, ...) | async-done | bytes 262160 | tf_op jit(solution)/shard_map/psum | solution.py:37
  379.2 0.8 constant_dynamic-update-slice_fusion.3
  380.0 0.8 constant_dynamic-update-slice_fusion.2
  380.9 0.8 constant_dynamic-update-slice_fusion.1
  381.7 0.8 constant_dynamic-update-slice_fusion
  384.1 1.2 reshape.369
  386.6 2.8 gather_fusion.1
  389.8 1.4 slice_bitcast_fusion.1
  394.3 1.4 copy.320
  396.0 1.0 convolution_bitcast_fusion.3
  397.0 1.0 convolution_bitcast_fusion.6
  398.5 1.8 fusion.15
  401.9 1.2 copy.517
  404.8 1.2 fusion.93
  406.6 0.9 concatenate.86
  408.6 0.9 concatenate.85
  409.5 1.2 pad_maximum_fusion.1
  410.7 2.5 broadcast_in_dim.69
  413.3 2.8 scatter_fusion
  416.1 9.7 %all-to-all-start.5 = ((bf16[64,32,1024]{2,1,0:T(8,128)(2,1)}), bf16[64,32,1024]{2,1,0:T(8,128)(2,1)}, u32[]{:S(2)}, u32[]{:S(2)}) async-start(bf16[64,32,1024]{2,1,0:T(8,128)(2,1)} %scatter_fusion), calls=%async_computation.5 | async-start | bytes 8388608 | tf_op jit(solution)/shard_map/all_to_all | solution.py:186
  426.4 1.4 copy.390
  427.8 1.4 reshape.434
  429.6 1.4 copy.393
  431.0 2.4 reshape.435
  433.5 1.1 copy-done.1
  434.8 1.4 collective-permute-start.3
  436.2 4.0 collective-permute-start.2
  441.9 1.0 collective-permute-done.2
  443.5 1.1 scatter-add.9
  444.6 206.4 %all-to-all-done.5 = bf16[64,32,1024]{2,1,0:T(8,128)(2,1)} async-done(((bf16[64,32,1024]{2,1,0:T(8,128)(2,1)}), bf16[64,32,1024]{2,1,0:T(8,128)(2,1)}, u32[]{:S(2)}, u32[]{:S(2)}) %all-to-all-start.5) | async-done | bytes 4194336 | tf_op jit(solution)/shard_map/all_to_all | solution.py:186
  651.0 6.7 fusion
  657.7 207.2 %all-gather.3.cloned.1.call-done = f32[256,32,1024]{2,1,0:T(8,128)} async-done(((f32[4,32,1024]{2,1,0:T(8,128)}), f32[256,32,1024]{2,1,0:T(8,128)}) %all-gather.3.cloned.1.call-update) | async-done | bytes 33554448 | tf_op jit(solution)/shard_map/all_gather | solution.py:16
  864.9 11.8 %reduce_sum.61 = f32[4,32,1024]{2,1,0:T(8,128)S(1)} reduce(f32[64,4,32,1024]{3,2,1,0:T(8,128)} %bitcast.224, f32[]{:T(128)} %constant.169.clone.1), dimensions={0}, to_apply=%region_10.11 | reduce | flops 8257536 | bytes 34078724 | tf_op jit(solution)/shard_map/reduce_sum | solution.py:16
  876.7 1.0 fusion.5
  (149 shorter events, 26.0 us)
Async XLA Ops:
  7.2 21.6 %copy-start.11 = (bf16[16,4096]{1,0:T(8,128)(2,1)S(1)}, bf16[16,4096]{1,0:T(8,128)(2,1)}, u32[]{:S(2)}) copy-start(bf16[16,4096]{1,0:T(8,128)(2,1)} %param.13) | copy-start | bytes 393220
  7.2 22.3 %copy-start.12 = (bf16[16,4096]{1,0:T(8,128)(2,1)S(1)}, bf16[16,4096]{1,0:T(8,128)(2,1)}, u32[]{:S(2)}) copy-start(bf16[16,4096]{1,0:T(8,128)(2,1)} %param.10) | copy-start | bytes 393220
  8.8 15.4 %all-to-all-start = ((bf16[16,8,512]{2,0,1:T(8,128)(2,1)}), bf16[16,8,512]{2,0,1:T(8,128)(2,1)S(1)}, u32[]{:S(2)}, u32[]{:S(2)}) async-start(bf16[16,8,512]{2,0,1:T(8,128)(2,1)} %bitcast.220), calls=%async_computation | async-start | bytes 262144 | tf_op jit(solution)/shard_map/all_to_all | solution.py:43
  23.9 14.3 %copy-start.13 = (s32[64]{0:T(128)}, s32[64]{0:T(128)S(1)}, u32[]{:S(2)}) copy-start(s32[64]{0:T(128)S(1)} %reduce_sum.57) | copy-start | bytes 772
  24.2 9.8 %all-to-all-start.1 = ((bf16[16,8,512]{2,0,1:T(8,128)(2,1)}), bf16[16,8,512]{2,0,1:T(8,128)(2,1)S(1)}, u32[]{:S(2)}, u32[]{:S(2)}) async-start(bf16[16,8,512]{2,0,1:T(8,128)(2,1)} %bitcast.219), calls=%async_computation.1 | async-start | bytes 262144 | tf_op jit(solution)/shard_map/all_to_all | solution.py:44
  34.0 9.4 %all-to-all-start.4 = ((bf16[16,8,512]{2,0,1:T(8,128)(2,1)}), bf16[16,8,512]{2,0,1:T(8,128)(2,1)S(1)}, u32[]{:S(2)}, u32[]{:S(2)}) async-start(bf16[16,8,512]{2,0,1:T(8,128)(2,1)} %bitcast.217), calls=%async_computation.4 | async-start | bytes 262144 | tf_op jit(solution)/shard_map/all_to_all | solution.py:45
  43.5 9.4 %all-to-all-start.3 = ((bf16[16,8,512]{2,0,1:T(8,128)(2,1)}), bf16[16,8,512]{2,0,1:T(8,128)(2,1)S(1)}, u32[]{:S(2)}, u32[]{:S(2)}) async-start(bf16[16,8,512]{2,0,1:T(8,128)(2,1)} %bitcast.218), calls=%async_computation.3 | async-start | bytes 262144 | tf_op jit(solution)/shard_map/all_to_all | solution.py:42
  52.3 15.0 %copy-start.19 = (s32[4]{0:T(128)S(1)}, s32[4]{0:T(128)}, u32[]{:S(2)}) copy-start(s32[4]{0:T(128)} %param.15) | copy-start | bytes 52
  52.9 333.7 %all-to-all-start.2 = ((bf16[64,32,1024]{2,1,0:T(8,128)(2,1)}), bf16[64,32,1024]{2,1,0:T(8,128)(2,1)}, u32[]{:S(2)}, u32[]{:S(2)}) async-start(bf16[64,32,1024]{2,1,0:T(8,128)(2,1)} %broadcast_select_fusion), calls=%async_computation.2 | async-start | bytes 8388608 | tf_op jit(solution)/shard_map/all_to_all | solution.py:88
  67.2 312.0 %all-reduce.5.cloned.1.call-start = ((), (), s32[]{:S(2)}) async-start(), calls=%async_computation.7 | async-start | bytes 524288 | tf_op jit(solution)/shard_map/psum | solution.py:37
  79.8 0.9 copy-start.16
  80.6 784.3 %all-gather.3.cloned.1.call-start = ((), (), s32[]{:S(2)}) async-start(), calls=%async_computation.6 | async-start | bytes 34078720 | tf_op jit(solution)/shard_map/all_gather | solution.py:16
  80.7 4.4 collective-permute-start
  83.5 5.6 collective-permute-start.1
  392.4 1.6 copy-start
  393.2 0.7 copy-start.6
  395.7 1.3 copy-start.10
  395.7 2.2 slice-start
  398.5 1.8 copy-start.4
  398.5 1.8 copy-start.8
  400.8 0.7 copy-start.7
  401.9 2.3 copy-start.2
  403.4 1.0 slice-start.1
  410.7 2.6 copy-start.17
  416.1 9.7 %copy-start.15 = (pred[256]{0:T(512)(128)(4,1)S(1)}, pred[256]{0:T(512)(128)(4,1)}, u32[]{:S(2)}) copy-start(pred[256]{0:T(512)(128)(4,1)} %get-tuple-element.33) | copy-start | bytes 772
  416.1 234.9 %all-to-all-start.5 = ((bf16[64,32,1024]{2,1,0:T(8,128)(2,1)}), bf16[64,32,1024]{2,1,0:T(8,128)(2,1)}, u32[]{:S(2)}, u32[]{:S(2)}) async-start(bf16[64,32,1024]{2,1,0:T(8,128)(2,1)} %scatter_fusion), calls=%async_computation.5 | async-start | bytes 8388608 | tf_op jit(solution)/shard_map/all_to_all | solution.py:186
  426.4 2.9 copy-start.5
  433.4 1.1 copy-start.1
  434.6 5.6 copy-start.3
  434.6 5.6 copy-start.9
  434.8 7.1 collective-permute-start.3
  436.2 6.7 collective-permute-start.2
  441.2 209.7 %copy-start.14 = (s32[64]{0:T(128)S(1)}, s32[64]{0:T(128)}, u32[]{:S(2)}) copy-start(s32[64]{0:T(128)} %copy-done.13) | copy-start | bytes 772
  864.9 11.8 %copy-start.18 = (pred[4]{0:T(512)(128)(4,1)S(1)}, pred[4]{0:T(512)(128)(4,1)}, u32[]{:S(2)}) copy-start(pred[4]{0:T(512)(128)(4,1)} %get-tuple-element.31) | copy-start | bytes 16
Sparse Core Ops, SparseCore 0:
  80.7 298.4 all-reduce.4
  404.4 460.4 all-gather.2
